TPU v7x, 32 devices: a whole 2x2x4 slice. The times are simulated.
32 devices in a mesh: req: 8 (over z, x), grp: 4 (over y, core).
Axes of the slice: x: 2, y: 2, z: 4, core: 2. Of those that a mesh axis runs over, the one named last changes fastest.
Arguments:
- residual: bfloat16 [8192, 2048], P('req', 'grp'), may hold values from -6 to 6
- queries: bfloat16 [8192, 2048], P('req', 'grp'), may hold values from -26 to 26
- new_keys: bfloat16 [8192, 512], P('req', 'grp'), may hold values from -26 to 26
- new_values: bfloat16 [8192, 512], P('req', 'grp'), may hold values from -6 to 6
- pool_keys: bfloat16 [36864, 512], P('req', 'grp'), may hold values from -6 to 6
- pool_values: bfloat16 [36864, 512], P('req', 'grp'), may hold values from -6 to 6
- cache_len: int32 [64], P('req'), may hold values from 1 to 512, as said below
- prefix_group: int32 [64], P('req'), may hold values from 0 to 7, as said below
- prefix_len: int32 [64], P('req'), may hold values from 0 to 512, as said below
- span_rows: int32 [8], replicated, may hold values from 0 to 1008, as said below
- span_offset: int32 [8], P('req'), may hold values from 0 to 512
- out_weight: bfloat16 [2048, 2048], P('grp'), may hold values from -0.125 to 0.125
- norm_gain: float32 [2048], replicated, may hold values from 0.1 to 1.9
- gate_weight: bfloat16 [2048, 4096], P(None, 'grp'), may hold values from -0.125 to 0.125
- up_weight: bfloat16 [2048, 4096], P(None, 'grp'), may hold values from -0.125 to 0.125
- down_weight: bfloat16 [4096, 2048], P('grp'), may hold values from -0.09375 to 0.09375
Outputs:
- layer_out: bfloat16 [8192, 2048], P('req', 'grp')
Inputs may be any that keep to these rules, and one draw needn't show every extreme that they name: `cache_len`: the first decode request of every req index has a cache of 512 positions. `prefix_group`: the slot, within its req index, of the first request of the group; at or before the request's own slot; a group's requests stand in consecutive slots. `prefix_len`: equal within a group and at most the cache length of each of its requests; some request shares 512 positions. `span_rows`: exactly 4 req indices hold a span of 1008 rows, the others none.
All inputs are finite; a program needn't handle non-finite values.
Results may differ from a plain program's by a relative error of at most 0.014.
Values may be sent and summed in bfloat16 or wider, within the bound.
No kernel may reach another device: no remote copies, remote signals or barrier semaphores. Data moves between devices by JAX's collectives and lax.ppermute only.
A program may use at most 128 MiB of HBM per device.

v0:
```python
import jax
import jax.numpy as jnp
from jax import lax
from jax.sharding import PartitionSpec as P

HEADS = 32
KV_HEADS = 8
HEAD_DIM = 64
DEC = 8
BAL = 512
REG = 512
MASKED_SCORE = -1e30


def attend(query_rows, key_rows, value_rows, allowed):
    scores = jnp.dot(query_rows, key_rows.T, preferred_element_type=jnp.float32) * query_rows.shape[
        1
    ] ** (-0.5)
    scores = jnp.where(allowed, scores, MASKED_SCORE)
    highest = jnp.max(scores, axis=1, keepdims=True)
    expval = jnp.exp(scores - highest)
    totals = jnp.sum(expval, axis=1, keepdims=True)
    probs = (expval / totals).astype(jnp.bfloat16)
    return jnp.dot(probs, value_rows, preferred_element_type=jnp.float32).astype(jnp.bfloat16)


def build_masks(cache_len, prefix_group, prefix_len, span_count, span_start, total_rows):
    position = jnp.arange(DEC * REG, dtype=jnp.int32)
    region = position // REG
    offset = position % REG
    request = jnp.arange(DEC, dtype=jnp.int32)
    shared = (region[None, :] == prefix_group[:, None]) & (offset[None, :] < prefix_len[:, None])
    owned = (
        (region[None, :] == request[:, None])
        & (offset[None, :] >= prefix_len[:, None])
        & (offset[None, :] < cache_len[:, None])
    )
    decode_mask = jnp.concatenate([shared | owned, jnp.eye(DEC, dtype=jnp.bool_)], axis=1)
    span_total = total_rows - DEC
    within = jnp.arange(span_total, dtype=jnp.int32)
    in_span = within < span_count
    earlier = jnp.arange(REG, dtype=jnp.int32)
    prior = (earlier[None, :] < span_start) & in_span[:, None]
    lowest = jnp.where(in_span, 0, within)
    causal = (within[None, :] >= lowest[:, None]) & (within[None, :] <= within[:, None])
    span_mask = jnp.concatenate([prior, causal], axis=1)
    return (decode_mask, span_mask)


def attention(queries, new_keys, new_values, pool_keys, pool_values, decode_mask, span_mask):
    head_count = queries.shape[1] // HEAD_DIM
    per_kv = HEADS // KV_HEADS
    split_at = DEC * REG

    def one_head(head):
        query_rows = lax.dynamic_slice_in_dim(queries, head * HEAD_DIM, HEAD_DIM, 1)
        column = head // per_kv * HEAD_DIM
        fresh_keys = lax.dynamic_slice_in_dim(new_keys, column, HEAD_DIM, 1)
        fresh_values = lax.dynamic_slice_in_dim(new_values, column, HEAD_DIM, 1)
        cached_keys = lax.dynamic_slice_in_dim(pool_keys, column, HEAD_DIM, 1)
        cached_values = lax.dynamic_slice_in_dim(pool_values, column, HEAD_DIM, 1)
        decode_out = attend(
            query_rows[:DEC],
            jnp.concatenate([cached_keys[:split_at], fresh_keys[:DEC]], axis=0),
            jnp.concatenate([cached_values[:split_at], fresh_values[:DEC]], axis=0),
            decode_mask,
        )
        span_out = attend(
            query_rows[DEC:],
            jnp.concatenate([cached_keys[split_at:], fresh_keys[DEC:]], axis=0),
            jnp.concatenate([cached_values[split_at:], fresh_values[DEC:]], axis=0),
            span_mask,
        )
        return jnp.concatenate([decode_out, span_out], axis=0)

    outputs = lax.map(one_head, jnp.arange(head_count, dtype=jnp.int32))
    return jnp.transpose(outputs, (1, 0, 2)).reshape(queries.shape[0], head_count * HEAD_DIM)


def finish(attn_rows, resid_rows, out_weight, norm_gain, gate_weight, up_weight, down_weight):
    partial_value = jnp.dot(attn_rows, out_weight, preferred_element_type=jnp.float32)
    proj_cols = lax.psum_scatter(
        partial_value.astype(jnp.bfloat16), "grp", scatter_dimension=1, tiled=True
    ).astype(jnp.float32)
    state_cols = (resid_rows.astype(jnp.float32) + proj_cols).astype(jnp.bfloat16)
    state_full = lax.all_gather(state_cols, "grp", axis=1, tiled=True)
    state32 = state_full.astype(jnp.float32)
    normed = (
        state32 * lax.rsqrt(jnp.mean(state32 * state32, axis=1, keepdims=True) + 1e-05) * norm_gain
    ).astype(jnp.bfloat16)
    gate = jnp.dot(normed, gate_weight, preferred_element_type=jnp.float32)
    upval = jnp.dot(normed, up_weight, preferred_element_type=jnp.float32)
    inner = (jax.nn.silu(gate) * upval).astype(jnp.bfloat16)
    down_cols = lax.psum_scatter(
        jnp.dot(inner, down_weight, preferred_element_type=jnp.float32).astype(jnp.bfloat16),
        "grp",
        scatter_dimension=1,
        tiled=True,
    ).astype(jnp.float32)
    return (state_cols.astype(jnp.float32) + down_cols).astype(jnp.bfloat16)


def shards(
    residual,
    queries,
    new_keys,
    new_values,
    pool_keys,
    pool_values,
    cache_len,
    prefix_group,
    prefix_len,
    span_rows,
    span_offset,
    out_weight,
    norm_gain,
    gate_weight,
    up_weight,
    down_weight,
):
    total_rows = residual.shape[0]
    width = residual.shape[1]
    device = lax.axis_index("req")
    devices = lax.axis_size("req")
    own_span = span_rows[device]
    decode_mask, span_mask = build_masks(
        cache_len, prefix_group, prefix_len, own_span, span_offset[0], total_rows
    )
    attn = attention(queries, new_keys, new_values, pool_keys, pool_values, decode_mask, span_mask)
    row_index = jnp.arange(total_rows, dtype=jnp.int32)
    is_live = row_index < DEC + own_span
    zero_value = jnp.zeros((), jnp.bfloat16)
    counts = DEC + span_rows
    first = jnp.sum(jnp.where(jnp.arange(devices, dtype=jnp.int32) < device, counts, 0))
    target = jnp.where(is_live, first + row_index, -1)
    bucket = (total_rows - DEC + devices - 1) // devices
    owner_dev = jnp.where(is_live, target % devices, devices)
    bucket_pos = jnp.where(is_live, row_index // devices, 0)
    send_attn = (
        jnp.zeros((devices, bucket, width), jnp.bfloat16)
        .at[owner_dev, bucket_pos]
        .set(attn, mode="drop")
    )
    send_resid = (
        jnp.zeros((devices, bucket, width), jnp.bfloat16)
        .at[owner_dev, bucket_pos]
        .set(residual, mode="drop")
    )
    send_target = (
        jnp.full((devices, bucket), -1, jnp.int32)
        .at[owner_dev, bucket_pos]
        .set(target, mode="drop")
    )
    got_attn, got_resid, got_target = (
        lax.all_to_all(send_attn, "req", split_axis=0, concat_axis=0, tiled=True),
        lax.all_to_all(send_resid, "req", split_axis=0, concat_axis=0, tiled=True),
        lax.all_to_all(send_target, "req", split_axis=0, concat_axis=0, tiled=True),
    )
    flat_target = got_target.reshape(-1)
    has_row = flat_target >= 0
    bal_slot = jnp.where(has_row, flat_target // devices, BAL)
    dense_attn = (
        jnp.zeros((BAL, width), jnp.bfloat16)
        .at[bal_slot]
        .set(got_attn.reshape(-1, width), mode="drop")
    )
    dense_resid = (
        jnp.zeros((BAL, width), jnp.bfloat16)
        .at[bal_slot]
        .set(got_resid.reshape(-1, width), mode="drop")
    )
    mixed = finish(
        dense_attn, dense_resid, out_weight, norm_gain, gate_weight, up_weight, down_weight
    )
    picked = jnp.where(has_row[:, None], mixed[jnp.minimum(bal_slot, BAL - 1)], zero_value)
    returned = lax.all_to_all(
        picked.reshape(devices, bucket, width), "req", split_axis=0, concat_axis=0, tiled=True
    )
    layer_out = jnp.where(
        is_live[:, None], returned[jnp.minimum(owner_dev, devices - 1), bucket_pos], zero_value
    )
    return layer_out


def solution(mesh):
    placed = (
        P("req", "grp"),
        P("req", "grp"),
        P("req", "grp"),
        P("req", "grp"),
        P("req", "grp"),
        P("req", "grp"),
        P("req"),
        P("req"),
        P("req"),
        P(),
        P("req"),
        P("grp", None),
        P(),
        P(None, "grp"),
        P(None, "grp"),
        P("grp", None),
    )
    return jax.shard_map(
        shards, mesh=mesh, in_specs=placed, out_specs=P("req", "grp"), check_vma=False
    )
```

profile of v0, /device:TPU:0, one launch (start us, length us, event | category | flops | bytes accessed | tf_op | source)
XLA Modules:
  0.0 414.9 jit_solution(9925079914877743265)
XLA Ops:
  13.4 4.3 %scatter_custom_fusion.2 = s32[1016]{0:T(1024)S(1)} fusion(s32[1024]{0:T(1024)S(1)} %get-tuple-element.165, s32[1024]{0:T(1024)S(1)} %add_select_fusion.1, s32[]{:T(128)} %constant.165.clone.1), kind=kCustom, calls=%fused_computation.122 | custom fusion | bytes 4068
  18.4 7.3 %all-to-all-start = ((s32[8,1,127]{2,1,0:T(1,128)}), s32[8,1,127]{2,1,0:T(1,128)}, u32[]{:S(2)}, u32[]{:S(2)}) async-start(s32[8,1,127]{2,1,0:T(1,128)} %bitcast.3), calls=%async_computation | async-start | bytes 8192 | tf_op jit(solution)/shard_map/all_to_all | solution.py:157
  32.1 151.4 %while.12 = (s32[]{:T(128)}, bf16[8,1024,64]{1,2,0:T(8,128)(2,1)}, s32[8]{0:T(128)}, bf16[1024,512]{1,0:T(8,128)(2,1)}, bf16[4608,128]{1,0:T(8,128)(2,1)S(1)}, /...) while((s32[]{:T(128)}, bf16[8,1024,64]{1,2,0:T(8,128)(2,1)}, ...), condition=%wide.region_9.10_spmd, body=%wide.region_4.9_spmd.sunk | while | flops 421723168 | bytes 31715728 | solution.py:76
  38.5 3.2 fusion.80
  43.2 2.2 fusion.82
  57.4 3.2 fusion.80
  76.4 3.2 fusion.80
  95.3 3.2 fusion.80
  114.2 3.2 fusion.80
  133.2 3.2 fusion.80
  137.9 2.2 fusion.82
  152.1 3.2 fusion.80
  171.0 3.2 fusion.80
  183.5 2.3 copy.35
  185.8 5.8 %scatter_custom_fusion.4 = bf16[1016,512]{1,0:T(8,128)(2,1)S(1)} fusion(s32[1024]{0:T(1024)} %get-tuple-element.164, bf16[1024,512]{1,0:T(8,128)(2,1)} %copy.35, bf16[]{:T(256)} %constant.170.clone.1), kind=kCustom, calls=%fused_computation.64 | custom fusion | bytes 1040896
  192.9 6.0 %all-to-all-start.2 = ((bf16[8,127,512]{2,1,0:T(8,128)(2,1)}), bf16[8,127,512]{2,1,0:T(8,128)(2,1)S(1)}, u32[]{:S(2)}, u32[]{:S(2)}) async-start(bf16[8,127,512]{2,1,0:T(8,128)(2,1)} %copy.36), calls=%async_computation.2 | async-start | bytes 2097152 | tf_op jit(solution)/shard_map/all_to_all | solution.py:155
  201.1 23.3 %all-to-all-done.2 = bf16[8,127,512]{2,1,0:T(8,128)(2,1)S(1)} async-done(((bf16[8,127,512]{2,1,0:T(8,128)(2,1)}), bf16[8,127,512]{2,1,0:T(8,128)(2,1)S(1)}, u32[]{:S(2)}, u32[]{:S(2)}) %all-to-all-start.2) | async-done | bytes 1040416 | tf_op jit(solution)/shard_map/all_to_all | solution.py:155
  225.6 6.3 %scatter_custom_fusion.1 = bf16[512,512]{1,0:T(8,128)(2,1)S(1)} fusion(s32[1016]{0:T(1024)S(1)} %bitcast.38, bf16[1016,512]{1,0:T(8,128)(2,1)} %reshape.365, bf16[]{:T(256)} %constant.170.clone.1), kind=kCustom, calls=%fused_computation.68 | custom fusion | bytes 524800 | tf_op jit(solution)/shard_map/scatter | solution.py:165
  232.0 2.6 convolution_convert_fusion.2
  234.7 5.8 %scatter_custom_fusion.3 = bf16[1016,512]{1,0:T(8,128)(2,1)S(1)} fusion(s32[1024]{0:T(1024)} %get-tuple-element.164, bf16[1024,512]{1,0:T(8,128)(2,1)} %param.18, bf16[]{:T(256)} %constant.170.clone.1), kind=kCustom, calls=%fused_computation.66 | custom fusion | bytes 1040896
  240.9 29.1 %all_to_all.24 = bf16[8,127,512]{2,1,0:T(8,128)(2,1)S(1)} all-to-all(bf16[8,127,512]{2,1,0:T(8,128)(2,1)S(1)} %copy.34), channel_id=1, replica_groups=mesh['req'=8,'grp'=4] {'req'}, dimensions={0} | all-to-all | bytes 2080768 | tf_op jit(solution)/shard_map/all_to_all | solution.py:156
  271.2 6.3 %scatter_custom_fusion = bf16[512,512]{1,0:T(8,128)(2,1)S(1)} fusion(s32[1016]{0:T(1024)S(1)} %bitcast.39, bf16[1016,512]{1,0:T(8,128)(2,1)} %reshape.357, bf16[]{:T(256)} %constant.170.clone.1), kind=kCustom, calls=%fused_computation.70 | custom fusion | bytes 524800 | tf_op jit(solution)/shard_map/scatter | solution.py:170
  279.9 21.6 %all-gather.2.cloned.1.call-done = bf16[512,2048]{1,0:T(8,128)(2,1)} async-done(((bf16[512,512]{1,0:T(8,128)(2,1)}), bf16[512,2048]{1,0:T(8,128)(2,1)}) %all-gather.2.cloned.1.call-update) | async-done | bytes 2097168 | tf_op jit(solution)/shard_map/all_gather | solution.py:86
  301.4 2.2 fusion.27
  303.7 5.9 %fusion.33 = f32[512,1024]{1,0:T(8,128)} fusion(bf16[2048,1024]{1,0:T(8,128)(2,1)} %param.31, bf16[512,2048]{1,0:T(8,128)(2,1)S(1)} %copy-done.6, f32[2048]{0:T(1024)S(1)} %copy-done.8, f32[512]{0:T(512)S(1)} %add_rsqrt_fusion), kind=kOutput, calls=%fused_computation.63 | convolution fusion | flops 2151677952 | bytes 8398848 | tf_op jit(solution)/shard_map/dot_general | solution.py:91
  309.6 10.6 %convolution_convert_fusion.1 = bf16[512,2048]{1,0:T(8,128)(2,1)} fusion(bf16[1024,2048]{1,0:T(8,128)(2,1)} %param.33, f32[512,1024]{1,0:T(8,128)} %fusion.33, bf16[2048,1024]{1,0:T(8,128)(2,1)} %param.32, bf16[512,2048]{1,0:T(8,128)(2,1)} %all-gather.2.cloned.1.call-done, f32[2048]{0:T(1024)S(1)} %copy-done.8, f32[512]{0:T(512)S(1)} %add_rsqrt_fusion), kind=kOutput, calls=%fused_computation.55 | convolution fusion | flops 4303355904 | bytes 14690304 | tf_op jit(solution)/shard_map/dot_general | solution.py:95
  321.0 30.8 %reduce-scatter.5.cloned.1.call-done = bf16[512,512]{1,0:T(8,128)(2,1)} async-done(((bf16[512,2048]{1,0:T(8,128)(2,1)}), bf16[512,512]{1,0:T(8,128)(2,1)}) %reduce-scatter.5.cloned.1.call-update) | async-done | bytes 524304 | tf_op jit(solution)/shard_map/reduce_scatter | solution.py:94
  353.0 5.1 %gather_fusion = bf16[1016,512]{1,0:T(8,128)(2,1)} fusion(bf16[512,512]{1,0:T(8,128)(2,1)S(1)} %add_convert_fusion, s32[1024]{0:T(1024)S(1)} %pad_clamp_fusion), kind=kCustom, calls=%fused_computation | custom fusion | bytes 2084832 | tf_op jit(solution)/shard_map/gather | solution.py:175
  360.8 5.5 %all-to-all-start.3 = ((bf16[8,127,512]{2,1,0:T(8,128)(2,1)}), bf16[8,127,512]{2,1,0:T(8,128)(2,1)}, u32[]{:S(2)}, u32[]{:S(2)}) async-start(bf16[8,127,512]{2,1,0:T(8,128)(2,1)} %broadcast_select_fusion.1), calls=%async_computation.5 | async-start | bytes 2097152 | tf_op jit(solution)/shard_map/all_to_all | solution.py:176
  367.0 25.2 %all-to-all-done.3 = bf16[8,127,512]{2,1,0:T(8,128)(2,1)} async-done(((bf16[8,127,512]{2,1,0:T(8,128)(2,1)}), bf16[8,127,512]{2,1,0:T(8,128)(2,1)}, u32[]{:S(2)}, u32[]{:S(2)}) %all-to-all-start.3) | async-done | bytes 1040416 | tf_op jit(solution)/shard_map/all_to_all | solution.py:176
  394.0 12.0 %gather_fusion.1 = bf16[1024,512]{1,0:T(8,128)(2,1)} fusion(bf16[8,127,512]{2,0,1:T(8,128)(2,1)S(1)} %copy.37, s32[1024]{0:T(1024)S(1)} %bitcast.33), kind=kCustom, calls=%fused_computation.1 | custom fusion | bytes 2105344 | tf_op jit(solution)/shard_map/gather | solution.py:180
  406.0 2.4 broadcast_select_fusion
  (217 shorter events, 121.3 us)
Async XLA Ops:
  6.5 225.5 %copy-start = (bf16[512,2048]{1,0:T(8,128)(2,1)S(1)}, bf16[512,2048]{1,0:T(8,128)(2,1)}, u32[]{:S(2)}) copy-start(bf16[512,2048]{1,0:T(8,128)(2,1)} %param.29) | copy-start | bytes 6291460
  18.4 174.6 %all-to-all-start = ((s32[8,1,127]{2,1,0:T(1,128)}), s32[8,1,127]{2,1,0:T(1,128)}, u32[]{:S(2)}, u32[]{:S(2)}) async-start(s32[8,1,127]{2,1,0:T(1,128)} %bitcast.3), calls=%async_computation | async-start | bytes 8192 | tf_op jit(solution)/shard_map/all_to_all | solution.py:157
  27.6 4.5 %copy-start.1 = (bf16[4608,128]{1,0:T(8,128)(2,1)S(1)}, bf16[4608,128]{1,0:T(8,128)(2,1)}, u32[]{:S(2)}) copy-start(bf16[4608,128]{1,0:T(8,128)(2,1)} %param.22) | copy-start | bytes 3538948
  27.6 4.5 %copy-start.3 = (bf16[1024,128]{1,0:T(8,128)(2,1)S(1)}, bf16[1024,128]{1,0:T(8,128)(2,1)}, u32[]{:S(2)}) copy-start(bf16[1024,128]{1,0:T(8,128)(2,1)} %param.20) | copy-start | bytes 786436
  41.8 1.0 copy-start.4
  41.8 1.4 copy-start.2
  45.5 0.8 copy-start.7
  60.7 1.0 copy-start.4
  60.7 1.4 copy-start.2
  64.4 0.8 copy-start.7
  79.6 1.0 copy-start.4
  79.6 1.4 copy-start.2
  83.3 0.8 copy-start.7
  98.5 1.0 copy-start.4
  98.5 1.4 copy-start.2
  117.5 1.0 copy-start.4
  117.5 1.4 copy-start.2
  136.4 1.0 copy-start.4
  136.4 1.4 copy-start.2
  140.1 0.8 copy-start.7
  155.3 1.0 copy-start.4
  155.3 1.4 copy-start.2
  174.2 1.0 copy-start.4
  174.3 1.4 copy-start.2
  192.9 31.4 %all-to-all-start.2 = ((bf16[8,127,512]{2,1,0:T(8,128)(2,1)}), bf16[8,127,512]{2,1,0:T(8,128)(2,1)S(1)}, u32[]{:S(2)}, u32[]{:S(2)}) async-start(bf16[8,127,512]{2,1,0:T(8,128)(2,1)} %copy.36), calls=%async_computation.2 | async-start | bytes 2097152 | tf_op jit(solution)/shard_map/all_to_all | solution.py:155
  198.9 78.7 %reduce-scatter.3.cloned.1.call-start = ((), (), s32[]{:S(2)}) async-start(), calls=%async_computation.6 | async-start | bytes 2621440 | tf_op jit(solution)/shard_map/reduce_scatter | solution.py:82
  234.7 66.8 %all-gather.2.cloned.1.call-start = ((), (), s32[]{:S(2)}) async-start(), calls=%async_computation.7 | async-start | bytes 2621440 | tf_op jit(solution)/shard_map/all_gather | solution.py:86
  277.6 26.1 %copy-start.8 = (f32[2048]{0:T(1024)S(1)}, f32[2048]{0:T(1024)}, u32[]{:S(2)}) copy-start(f32[2048]{0:T(1024)} %param.30) | copy-start | bytes 24580
  279.6 72.3 %reduce-scatter.5.cloned.1.call-start = ((), (), s32[]{:S(2)}) async-start(), calls=%async_computation.8 | async-start | bytes 2621440 | tf_op jit(solution)/shard_map/reduce_scatter | solution.py:94
  301.4 2.2 copy-start.6
  320.2 31.6 %copy-start.5 = (bf16[512,512]{1,0:T(8,128)(2,1)S(1)}, bf16[512,512]{1,0:T(8,128)(2,1)}, u32[]{:S(2)}) copy-start(bf16[512,512]{1,0:T(8,128)(2,1)} %add_convert_fusion.1) | copy-start | bytes 1572868
  360.8 31.4 %all-to-all-start.3 = ((bf16[8,127,512]{2,1,0:T(8,128)(2,1)}), bf16[8,127,512]{2,1,0:T(8,128)(2,1)}, u32[]{:S(2)}, u32[]{:S(2)}) async-start(bf16[8,127,512]{2,1,0:T(8,128)(2,1)} %broadcast_select_fusion.1), calls=%async_computation.5 | async-start | bytes 2097152 | tf_op jit(solution)/shard_map/all_to_all | solution.py:176
  (4 other events, 3.0 us)
Sparse Core Ops, SparseCore 0:
  234.8 30.2 reduce-scatter.2
  279.7 21.6 all-gather.1
  320.4 31.4 reduce-scatter.4
where the time goes:
time: 418 us; the launch traced here: 415 us
  waiting for transfers between devices  101 us (24%)
  local copies, waits for them, and re-layouts  98.6 us (24%)
  matrix products  79.5 us (19%)
  other arithmetic  44.7 us (11%)
  blocking collectives  29.1 us (7%)
  loops' own time  28.2 us (7%)
  starting transfers between devices  19.1 us (5%)
  between operations  14.8 us (4%)
    dot_general x16, matrix products, attend(): jnp.dot(query_rows, key_rows.T, preferred_element_type=jnp.float32)  35.5 us
    reduce_scatter x1, waiting for transfers between devices, finish(): lax.psum_scatter(jnp.dot(inner, down_weight, preferred_element_type=jnp.f...  30.8 us
    all_to_all x1, blocking collectives, shards(): lax.all_to_all(send_resid, 'req', split_axis=0, concat_axis=0, tiled=True)  29.1 us
    another operation x1, loops' own time, attention(): outputs = lax.map(one_head, jnp.arange(head_count, dtype=jnp.int32))  28.2 us
    all_to_all x1, waiting for transfers between devices, shards(): lax.all_to_all(picked.reshape(devices, bucket, width), 'req', split_axis=...  25.2 us
    dot_general x16, matrix products, attend(): jnp.dot(probs, value_rows, preferred_element_type=jnp.float32)  24.8 us
    all_to_all x1, waiting for transfers between devices, shards(): lax.all_to_all(send_attn, 'req', split_axis=0, concat_axis=0, tiled=True)  23.3 us
    all_gather x1, waiting for transfers between devices, finish(): state_full = lax.all_gather(state_cols, 'grp', axis=1, tiled=True)  21.6 us
  transfers between devices with their start and end apart: 6, of which 4 were waited for; matrix products, arithmetic and copies ran while one was open for 37% of the time, Pallas kernels for 0%

commit v1 on v0

--- a/solution.py
+++ b/solution.py
@@ -83,7 +83,15 @@
         partial_value.astype(jnp.bfloat16), "grp", scatter_dimension=1, tiled=True
     ).astype(jnp.float32)
     state_cols = (resid_rows.astype(jnp.float32) + proj_cols).astype(jnp.bfloat16)
-    state_full = lax.all_gather(state_cols, "grp", axis=1, tiled=True)
+    ways, here = (lax.axis_size("grp"), lax.axis_index("grp"))
+    grown, reach = (state_cols, 1)
+    while reach < ways:
+        theirs = lax.ppermute(grown, "grp", [(d, d ^ reach) for d in range(ways)])
+        mine_first = jnp.concatenate([grown, theirs], axis=1)
+        theirs_first = jnp.concatenate([theirs, grown], axis=1)
+        grown = jnp.where(here & reach == 0, mine_first, theirs_first)
+        reach = 2 * reach
+    state_full = grown
     state32 = state_full.astype(jnp.float32)
     normed = (
         state32 * lax.rsqrt(jnp.mean(state32 * state32, axis=1, keepdims=True) + 1e-05) * norm_gain

time: 418 us -> 426 us (1.019)
    ppermute x0 -> x2, waiting for transfers between devices: none -> 25.9 us  [finish(): theirs = lax.ppermute(grown, 'grp', [(d, d ^ reach) for d in range(ways)])]
    all_gather x1 -> x0, waiting for transfers between devices: 21.6 us -> none  [finish(): state_full = lax.all_gather(state_cols, 'grp', axis=1, tiled=True)]
    unnamed x15 -> x11, local copies, waits for them, and re-layouts: 16 us -> 16 us
  transfers between devices with their start and end apart: 6 -> 7, of which waited for: 4 -> 5; matrix products, arithmetic and copies ran while one was open for 37% -> 36% of each run, Pallas kernels for 0% -> 0%
where the time goes in v1:
time: 426 us; the launch traced here: 423 us
  waiting for transfers between devices  104 us (24%)
  local copies, waits for them, and re-layouts  98.8 us (23%)
  matrix products  81.4 us (19%)
  other arithmetic  45.9 us (11%)
  blocking collectives  29.1 us (7%)
  loops' own time  28.2 us (7%)
  starting transfers between devices  20.4 us (5%)
  between operations  15.1 us (4%)
    dot_general x16, matrix products, attend(): jnp.dot(query_rows, key_rows.T, preferred_element_type=jnp.float32)  35.5 us
    reduce_scatter x1, waiting for transfers between devices, finish(): lax.psum_scatter(jnp.dot(inner, down_weight, preferred_element_type=jnp.f...  30 us
    all_to_all x1, blocking collectives, shards(): lax.all_to_all(send_resid, 'req', split_axis=0, concat_axis=0, tiled=True)  29.1 us
    another operation x1, loops' own time, attention(): outputs = lax.map(one_head, jnp.arange(head_count, dtype=jnp.int32))  28.2 us
    ppermute x2, waiting for transfers between devices, finish(): theirs = lax.ppermute(grown, 'grp', [(d, d ^ reach) for d in range(ways)])  25.9 us
    all_to_all x1, waiting for transfers between devices, shards(): lax.all_to_all(picked.reshape(devices, bucket, width), 'req', split_axis=...  25.2 us
    dot_general x16, matrix products, attend(): jnp.dot(probs, value_rows, preferred_element_type=jnp.float32)  24.8 us
    all_to_all x1, waiting for transfers between devices, shards(): lax.all_to_all(send_attn, 'req', split_axis=0, concat_axis=0, tiled=True)  23.3 us
  transfers between devices with their start and end apart: 7, of which 5 were waited for; matrix products, arithmetic and copies ran while one was open for 36% of the time, Pallas kernels for 0%

profile of v1, /device:TPU:0, one launch (start us, length us, event | category | flops | bytes accessed | tf_op | source)
XLA Modules:
  0.0 423.4 jit_solution(845612251730111521)
XLA Ops:
  13.4 4.3 %scatter_custom_fusion.2 = s32[1016]{0:T(1024)S(1)} fusion(s32[1024]{0:T(1024)S(1)} %get-tuple-element.165, s32[1024]{0:T(1024)S(1)} %add_select_fusion.1, s32[]{:T(128)} %constant.169.clone.1), kind=kCustom, calls=%fused_computation.124 | custom fusion | bytes 4068
  18.4 7.3 %all-to-all-start = ((s32[8,1,127]{2,1,0:T(1,128)}), s32[8,1,127]{2,1,0:T(1,128)}, u32[]{:S(2)}, u32[]{:S(2)}) async-start(s32[8,1,127]{2,1,0:T(1,128)} %bitcast.3), calls=%async_computation | async-start | bytes 8192 | tf_op jit(solution)/shard_map/all_to_all | solution.py:165
  32.2 151.4 %while.12 = (s32[]{:T(128)}, bf16[8,1024,64]{1,2,0:T(8,128)(2,1)}, s32[8]{0:T(128)}, bf16[1024,512]{1,0:T(8,128)(2,1)}, bf16[4608,128]{1,0:T(8,128)(2,1)S(1)}, /...) while((s32[]{:T(128)}, bf16[8,1024,64]{1,2,0:T(8,128)(2,1)}, ...), condition=%wide.region_9.10_spmd, body=%wide.region_4.9_spmd.sunk | while | flops 421723168 | bytes 31715728 | solution.py:76
  38.6 3.2 fusion.80
  43.3 2.2 fusion.82
  57.5 3.2 fusion.80
  76.4 3.2 fusion.80
  95.3 3.2 fusion.80
  100.1 2.2 fusion.82
  114.3 3.2 fusion.80
  133.2 3.2 fusion.80
  152.1 3.2 fusion.80
  171.0 3.2 fusion.80
  183.6 2.3 copy.35
  185.9 5.8 %scatter_custom_fusion.4 = bf16[1016,512]{1,0:T(8,128)(2,1)S(1)} fusion(s32[1024]{0:T(1024)} %get-tuple-element.164, bf16[1024,512]{1,0:T(8,128)(2,1)} %copy.35, bf16[]{:T(256)} %constant.174.clone.1), kind=kCustom, calls=%fused_computation.66 | custom fusion | bytes 1040896
  193.0 6.0 %all-to-all-start.2 = ((bf16[8,127,512]{2,1,0:T(8,128)(2,1)}), bf16[8,127,512]{2,1,0:T(8,128)(2,1)S(1)}, u32[]{:S(2)}, u32[]{:S(2)}) async-start(bf16[8,127,512]{2,1,0:T(8,128)(2,1)} %copy.36), calls=%async_computation.2 | async-start | bytes 2097152 | tf_op jit(solution)/shard_map/all_to_all | solution.py:163
  201.1 23.3 %all-to-all-done.2 = bf16[8,127,512]{2,1,0:T(8,128)(2,1)S(1)} async-done(((bf16[8,127,512]{2,1,0:T(8,128)(2,1)}), bf16[8,127,512]{2,1,0:T(8,128)(2,1)S(1)}, u32[]{:S(2)}, u32[]{:S(2)}) %all-to-all-start.2) | async-done | bytes 1040416 | tf_op jit(solution)/shard_map/all_to_all | solution.py:163
  225.7 6.3 %scatter_custom_fusion.1 = bf16[512,512]{1,0:T(8,128)(2,1)S(1)} fusion(s32[1016]{0:T(1024)S(1)} %bitcast.38, bf16[1016,512]{1,0:T(8,128)(2,1)} %reshape.365, bf16[]{:T(256)} %constant.174.clone.1), kind=kCustom, calls=%fused_computation.70 | custom fusion | bytes 524800 | tf_op jit(solution)/shard_map/scatter | solution.py:173
  232.1 2.6 convolution_convert_fusion.2
  234.7 5.8 %scatter_custom_fusion.3 = bf16[1016,512]{1,0:T(8,128)(2,1)S(1)} fusion(s32[1024]{0:T(1024)} %get-tuple-element.164, bf16[1024,512]{1,0:T(8,128)(2,1)} %param.18, bf16[]{:T(256)} %constant.174.clone.1), kind=kCustom, calls=%fused_computation.68 | custom fusion | bytes 1040896
  240.9 29.1 %all_to_all.24 = bf16[8,127,512]{2,1,0:T(8,128)(2,1)S(1)} all-to-all(bf16[8,127,512]{2,1,0:T(8,128)(2,1)S(1)} %copy.34), channel_id=1, replica_groups=mesh['req'=8,'grp'=4] {'req'}, dimensions={0} | all-to-all | bytes 2080768 | tf_op jit(solution)/shard_map/all_to_all | solution.py:164
  271.2 6.6 %scatter_custom_fusion = bf16[512,512]{1,0:T(8,128)(2,1)S(1)} fusion(s32[1016]{0:T(1024)S(1)} %bitcast.39, bf16[1016,512]{1,0:T(8,128)(2,1)} %reshape.357, bf16[]{:T(256)} %constant.174.clone.1), kind=kCustom, calls=%fused_computation.72 | custom fusion | bytes 524800 | tf_op jit(solution)/shard_map/scatter | solution.py:178
  283.8 24.0 %collective-permute-done.1 = bf16[512,1024]{1,0:T(8,128)(2,1)} collective-permute-done((bf16[512,1024]{1,0:T(8,128)(2,1)}, bf16[512,1024]{1,0:T(8,128)(2,1)}, u32[]{:S(2)}, u32[]{:S(2)}) %collective-permute-start.1) | collective-permute-done | bytes 1048608 | tf_op jit(solution)/shard_map/ppermute | solution.py:89
  307.8 3.0 fusion.27
  310.8 7.2 %fusion.33 = f32[512,1024]{1,0:T(8,128)} fusion(bf16[2048,1024]{1,0:T(8,128)(2,1)} %param.31, f32[2048]{0:T(1024)S(1)} %copy-done.6, f32[512]{0:T(512)S(1)} %add_rsqrt_fusion, bf16[512,1024]{1,0:T(8,128)(2,1)} %collective-permute-done.1, bf16[512,1024]{1,0:T(8,128)(2,1)} %maximum_select_fusion.1, pred[]{:T(512)S(6)} %eq.45), kind=kOutput, calls=%fused_computation.65 | convolution fusion | flops 2161115136 | bytes 8398849 | tf_op jit(solution)/shard_map/dot_general | solution.py:99
  318.0 11.3 %convolution_convert_fusion.1 = bf16[512,2048]{1,0:T(8,128)(2,1)} fusion(bf16[1024,2048]{1,0:T(8,128)(2,1)} %param.33, f32[512,1024]{1,0:T(8,128)} %fusion.33, bf16[2048,1024]{1,0:T(8,128)(2,1)} %param.32, f32[2048]{0:T(1024)S(1)} %copy-done.6, f32[512]{0:T(512)S(1)} %add_rsqrt_fusion, bf16[512,1024]{1,0:T(8,128)(2,1)} %collective-permute-done.1, ...), kind=kOutput, calls=%fused_computation.55 | convolution fusion | flops 4312793088 | bytes 14690305 | tf_op jit(solution)/shard_map/dot_general | solution.py:103
  330.0 30.0 %reduce-scatter.5.cloned.1.call-done = bf16[512,512]{1,0:T(8,128)(2,1)} async-done(((bf16[512,2048]{1,0:T(8,128)(2,1)}), bf16[512,512]{1,0:T(8,128)(2,1)}) %reduce-scatter.5.cloned.1.call-update) | async-done | bytes 524304 | tf_op jit(solution)/shard_map/reduce_scatter | solution.py:102
  361.2 5.1 %gather_fusion = bf16[1016,512]{1,0:T(8,128)(2,1)} fusion(bf16[512,512]{1,0:T(8,128)(2,1)S(1)} %add_convert_fusion, s32[1024]{0:T(1024)S(1)} %pad_clamp_fusion), kind=kCustom, calls=%fused_computation | custom fusion | bytes 2084832 | tf_op jit(solution)/shard_map/gather | solution.py:183
  369.0 5.5 %all-to-all-start.3 = ((bf16[8,127,512]{2,1,0:T(8,128)(2,1)}), bf16[8,127,512]{2,1,0:T(8,128)(2,1)}, u32[]{:S(2)}, u32[]{:S(2)}) async-start(bf16[8,127,512]{2,1,0:T(8,128)(2,1)} %broadcast_select_fusion.1), calls=%async_computation.5 | async-start | bytes 2097152 | tf_op jit(solution)/shard_map/all_to_all | solution.py:184
  375.2 25.2 %all-to-all-done.3 = bf16[8,127,512]{2,1,0:T(8,128)(2,1)} async-done(((bf16[8,127,512]{2,1,0:T(8,128)(2,1)}), bf16[8,127,512]{2,1,0:T(8,128)(2,1)}, u32[]{:S(2)}, u32[]{:S(2)}) %all-to-all-start.3) | async-done | bytes 1040416 | tf_op jit(solution)/shard_map/all_to_all | solution.py:184
  402.2 12.0 %gather_fusion.1 = bf16[1024,512]{1,0:T(8,128)(2,1)} fusion(bf16[8,127,512]{2,0,1:T(8,128)(2,1)S(1)} %copy.37, s32[1024]{0:T(1024)S(1)} %bitcast.33), kind=kCustom, calls=%fused_computation.1 | custom fusion | bytes 2105344 | tf_op jit(solution)/shard_map/gather | solution.py:188
  414.1 2.4 broadcast_select_fusion
  (215 shorter events, 124.8 us)
Async XLA Ops:
  6.5 225.5 %copy-start = (bf16[512,2048]{1,0:T(8,128)(2,1)S(1)}, bf16[512,2048]{1,0:T(8,128)(2,1)}, u32[]{:S(2)}) copy-start(bf16[512,2048]{1,0:T(8,128)(2,1)} %param.29) | copy-start | bytes 6291460
  18.4 174.6 %all-to-all-start = ((s32[8,1,127]{2,1,0:T(1,128)}), s32[8,1,127]{2,1,0:T(1,128)}, u32[]{:S(2)}, u32[]{:S(2)}) async-start(s32[8,1,127]{2,1,0:T(1,128)} %bitcast.3), calls=%async_computation | async-start | bytes 8192 | tf_op jit(solution)/shard_map/all_to_all | solution.py:165
  27.6 4.5 %copy-start.1 = (bf16[4608,128]{1,0:T(8,128)(2,1)S(1)}, bf16[4608,128]{1,0:T(8,128)(2,1)}, u32[]{:S(2)}) copy-start(bf16[4608,128]{1,0:T(8,128)(2,1)} %param.22) | copy-start | bytes 3538948
  27.7 4.5 %copy-start.3 = (bf16[1024,128]{1,0:T(8,128)(2,1)S(1)}, bf16[1024,128]{1,0:T(8,128)(2,1)}, u32[]{:S(2)}) copy-start(bf16[1024,128]{1,0:T(8,128)(2,1)} %param.20) | copy-start | bytes 786436
  41.8 1.0 copy-start.4
  41.8 1.4 copy-start.2
  45.5 0.8 copy-start.5
  60.7 1.0 copy-start.4
  60.7 1.4 copy-start.2
  64.4 0.8 copy-start.5
  79.6 1.0 copy-start.4
  79.7 1.4 copy-start.2
  83.4 0.8 copy-start.5
  98.6 1.0 copy-start.4
  98.6 1.4 copy-start.2
  102.3 0.8 copy-start.5
  117.5 1.0 copy-start.4
  117.5 1.4 copy-start.2
  121.2 0.8 copy-start.5
  136.4 1.0 copy-start.4
  136.4 1.4 copy-start.2
  155.4 1.0 copy-start.4
  155.4 1.4 copy-start.2
  174.3 1.0 copy-start.4
  174.3 1.4 copy-start.2
  193.0 31.4 %all-to-all-start.2 = ((bf16[8,127,512]{2,1,0:T(8,128)(2,1)}), bf16[8,127,512]{2,1,0:T(8,128)(2,1)S(1)}, u32[]{:S(2)}, u32[]{:S(2)}) async-start(bf16[8,127,512]{2,1,0:T(8,128)(2,1)} %copy.36), calls=%async_computation.2 | async-start | bytes 2097152 | tf_op jit(solution)/shard_map/all_to_all | solution.py:163
  199.0 78.9 %reduce-scatter.3.cloned.1.call-start = ((), (), s32[]{:S(2)}) async-start(), calls=%async_computation.6 | async-start | bytes 2621440 | tf_op jit(solution)/shard_map/reduce_scatter | solution.py:82
  234.7 125.3 %reduce-scatter.5.cloned.1.call-start = ((), (), s32[]{:S(2)}) async-start(), calls=%async_computation.7 | async-start | bytes 2621440 | tf_op jit(solution)/shard_map/reduce_scatter | solution.py:102
  279.0 2.0 collective-permute-start
  279.1 31.7 %copy-start.6 = (f32[2048]{0:T(1024)S(1)}, f32[2048]{0:T(1024)}, u32[]{:S(2)}) copy-start(f32[2048]{0:T(1024)} %param.30) | copy-start | bytes 24580
  282.3 25.5 %collective-permute-start.1 = (bf16[512,1024]{1,0:T(8,128)(2,1)}, bf16[512,1024]{1,0:T(8,128)(2,1)}, u32[]{:S(2)}, u32[]{:S(2)}) collective-permute-start(bf16[512,1024]{1,0:T(8,128)(2,1)} %maximum_select_fusion.1), channel_id=1, source_target_pairs={{0,2},{1,3},{2,0},{3,1},{4,6},{5,7},{6,4},{7,5},{8,10},{9,11},{10,... | collective-permute-start | bytes 3145736 | tf_op jit(solution)/shard_map/ppermute | solution.py:89
  369.0 31.4 %all-to-all-start.3 = ((bf16[8,127,512]{2,1,0:T(8,128)(2,1)}), bf16[8,127,512]{2,1,0:T(8,128)(2,1)}, u32[]{:S(2)}, u32[]{:S(2)}) async-start(bf16[8,127,512]{2,1,0:T(8,128)(2,1)} %broadcast_select_fusion.1), calls=%async_computation.5 | async-start | bytes 2097152 | tf_op jit(solution)/shard_map/all_to_all | solution.py:184
  (3 other events, 2.3 us)
Sparse Core Ops, SparseCore 0:
  234.8 30.2 reduce-scatter.2
  329.4 30.4 reduce-scatter.4
